TPU v7x, 512 devices: a whole 4x4x16 slice. The times are simulated.
512 devices in a mesh: dp: 4 (over x), seq: 8 (over z_lo), tensor: 16 (over z_hi, y, core).
Axes of the slice: x: 4, y: 4, z: 16 (z_hi: 2, z_lo: 8; z = z_hi * 8 + z_lo), core: 2. Of those that a mesh axis runs over, the one named last changes fastest.
Arguments:
- features: bfloat16 [4096, 4096], P(('dp', 'seq'), 'tensor'), parts along dimension 0, may hold values from -6 to 6
- in_weight: bfloat16 [4096, 3, 4096], P('seq', None, 'tensor'), may hold values from -0.09375 to 0.09375
- short_taps: float32 [3, 7, 4096], P(None, None, 'tensor'), may hold values from -2.5 to 2.5
- decay_rates: float32 [16, 4096], P(None, 'tensor'), may hold values from 0.00048828125 to 0.1
- residues: float32 [16, 4096], P(None, 'tensor'), may hold values from -1.5 to 1.5
- skip_gain: float32 [4096], P('tensor'), may hold values from 0.5 to 1.5
- out_weight: bfloat16 [4096, 4096], P(None, 'tensor'), may hold values from -0.09375 to 0.09375
Outputs:
- mixed: bfloat16 [4096, 4096], P(('dp', 'seq'), 'tensor'), parts along dimension 0
There are 4 independent parts, one for each index of `dp`. A program takes and returns all parts, laid end to end along the dimension named above; an argument that names none is the same for every part. Nothing has to cross between parts.
All inputs are finite; a program needn't handle non-finite values.
Results may differ from a plain program's by a relative error of at most 0.007.
Values may be sent and summed in bfloat16 or wider, within the bound.
No kernel may reach another device: no remote copies, remote signals or barrier semaphores. Data moves between devices by JAX's collectives and lax.ppermute only.
A program may use at most 64 MiB of HBM per device.

v0:
```python
import jax
import jax.numpy as jnp
from jax import lax
from jax.sharding import PartitionSpec as P

precise = lax.Precision.HIGHEST
block_len = 64


def passed_along(value, axis, steps):
    count = lax.axis_size(axis)
    leading, last = (max(0, -steps), min(count, count - steps))
    return lax.ppermute(value, axis, [(source, source + steps) for source in range(leading, last)])


def prefix_2(part, axis, combine, identity):
    place = lax.axis_index(axis)
    gathered = jax.tree.map(lambda a: lax.all_gather(a, axis), part)
    state = jax.tree.map(lambda a, e: jnp.zeros_like(a) + jnp.asarray(e, a.dtype), part, identity)

    def one(turn, state):
        return combine(
            state, jax.tree.map(lambda a: lax.dynamic_index_in_dim(a, turn, 0, False), gathered)
        )

    return lax.fori_loop(0, place, one, state)


def body(features, in_weight, short_taps, decay_rates, residues, skip_gain, out_weight):
    tok_rows = features.shape[0]
    channels = in_weight.shape[2]
    taps_count = short_taps.shape[1]
    whole_feats = lax.all_gather(features, "tensor", axis=1, tiled=True)
    piece = lax.all_gather(in_weight, "seq", axis=0, tiled=True)
    count = piece.shape[0]
    projected = jnp.dot(
        whole_feats, piece.reshape(count, 3 * channels), preferred_element_type=jnp.float32
    )
    projected = projected.astype(jnp.bfloat16).reshape(tok_rows, 3, channels)
    rim_rows = taps_count - 1
    earlier = passed_along(projected[tok_rows - rim_rows :], "seq", 1)
    extended = jnp.concatenate([earlier, projected], axis=0).astype(jnp.float32)
    short = jnp.zeros((tok_rows, 3, channels), jnp.float32)
    for offset_lag in range(taps_count):
        short = (
            short
            + short_taps[:, offset_lag, :][None]
            * extended[rim_rows - offset_lag : rim_rows - offset_lag + tok_rows]
        )
    product = short[:, 1, :] * short[:, 2, :]
    blocks = tok_rows // block_len
    pieces = product.reshape(blocks, block_len, channels)
    amplitude = residues * jnp.sqrt(2.0 * decay_rates)
    offsets = jnp.arange(block_len).astype(jnp.float32)
    falloff = jnp.exp(-decay_rates[:, None, :] * offsets[None, :, None])
    kernel = jnp.einsum("mc,mtc->tc", amplitude, falloff, precision=precise)
    lag_grid = jnp.arange(block_len)[:, None] - jnp.arange(block_len)[None, :]
    select = (lag_grid[:, :, None] == jnp.arange(block_len)[None, None, :]).astype(jnp.float32)
    toeplitz = jnp.einsum("tsk,kc->tsc", select, kernel, precision=precise)
    inner = jnp.einsum("tsc,bsc->btc", toeplitz, pieces, precision=precise)
    toward_end = jnp.exp(-decay_rates[:, None, :] * (block_len - offsets)[None, :, None])
    block_sums = jnp.einsum("msc,bsc->bmc", toward_end, pieces, precision=precise)
    block_index = jnp.arange(blocks).astype(jnp.float32)
    carry_over = jnp.exp(
        -decay_rates[None] * (block_len * (blocks - 1 - block_index))[:, None, None]
    )
    device_sum = jnp.sum(carry_over * block_sums, axis=0)
    device_decay = jnp.exp(-decay_rates * float(tok_rows))

    def combine(earlier_pair, later_pair):
        return (earlier_pair[0] * later_pair[0], later_pair[0] * earlier_pair[1] + later_pair[1])

    prefix = prefix_2(
        (device_decay, device_sum),
        "seq",
        combine,
        (jnp.ones_like(device_decay), jnp.zeros_like(device_sum)),
    )
    entering = prefix[1]
    step_decay = jnp.exp(-decay_rates * float(block_len))

    def advance(state, block_sum):
        return (step_decay * state + block_sum, state)

    final_state, starts = lax.scan(advance, entering, block_sums)
    outer = jnp.einsum("mic,bmc->bic", amplitude[:, None, :] * falloff, starts, precision=precise)
    conv = (inner + outer).reshape(tok_rows, channels)
    gated = (short[:, 0, :] * (conv + skip_gain[None, :] * product)).astype(jnp.bfloat16)
    mixed = jnp.dot(
        lax.all_gather(gated, "tensor", axis=1, tiled=True),
        out_weight,
        preferred_element_type=jnp.float32,
    )
    return mixed.astype(jnp.bfloat16)


def solution(mesh):
    in_specs = (
        P(("dp", "seq"), "tensor"),
        P("seq", None, "tensor"),
        P(None, None, "tensor"),
        P(None, "tensor"),
        P(None, "tensor"),
        P("tensor"),
        P(None, "tensor"),
    )
    out_specs = P(("dp", "seq"), "tensor")
    return jax.shard_map(body, mesh=mesh, in_specs=in_specs, out_specs=out_specs, check_vma=False)
```

profile of v0, /device:TPU:1, one launch (start us, length us, event | category | flops | bytes accessed | tf_op | source)
XLA Modules:
  0.0 453.0 jit_solution(18063631675276910231)
XLA Ops:
  6.5 0.0 copy-start
  6.5 0.0 all-gather.6.cloned.1.call-start
  6.6 0.7 all-gather.6.cloned.1.call-update
  7.3 0.0 all-gather.8.cloned.1.call-start
  7.3 2.3 copy.59
  9.7 0.0 all-gather.8.cloned.1.call-update
  9.7 0.0 all-gather.10.cloned.1.call-start
  9.7 0.0 copy-done.4
  9.7 0.0 copy-done.5
  9.8 0.1 copy.90
  9.9 0.1 copy.63
  10.0 0.0 copy-start.7
  10.0 0.5 subtract_multiply_fusion
  10.5 0.5 broadcast_subtract_fusion
  11.1 1.6 multiply_reduce_fusion
  12.7 0.0 copy-done.3
  12.8 3.8 fusion.5
  16.6 76.7 %all-gather.6.cloned.1.call-done = bf16[128,4096]{1,0:T(8,128)(2,1)} async-done(((bf16[128,256]{1,0:T(8,128)(2,1)}), bf16[128,4096]{1,0:T(8,128)(2,1)}) %all-gather.6.cloned.1.call-update) | async-done | bytes 1048592 | tf_op jit(solution)/shard_map/all_gather | solution.py:33
  93.3 135.5 %all-gather.8.cloned.1.call-done = bf16[4096,3,256]{0,2,1:T(8,128)(2,1)} async-done(((bf16[512,3,256]{0,2,1:T(8,128)(2,1)}), bf16[4096,3,256]{0,2,1:T(8,128)(2,1)}) %all-gather.8.cloned.1.call-update) | async-done | bytes 6291472 | tf_op jit(solution)/shard_map/all_gather | solution.py:34
  228.8 5.3 %convolution_convert_fusion = bf16[128,768]{1,0:T(8,128)(2,1)S(1)} fusion(bf16[128,4096]{1,0:T(8,128)(2,1)} %all-gather.6.cloned.1.call-done, bf16[4096,768]{0,1:T(8,128)(2,1)} %bitcast.70), kind=kOutput, calls=%fused_computation.13 | convolution fusion | flops 805404672 | bytes 7536640 | tf_op jit(solution)/shard_map/dot_general | solution.py:36
  234.2 0.2 copy.81
  234.4 1.3 collective-permute-start
  235.7 40.2 %all-gather = f32[128,256]{1,0:T(8,128)S(1)} all-gather(f32[16,256]{1,0:T(8,128)S(1)} %get-tuple-element.136), channel_id=2, replica_groups=mesh['dp'=4,'seq'=8,'tensor'=16] {'seq'}, dimensions={0}, use_global_device_ids=true | all-gather | bytes 147456 | tf_op jit(solution)/shard_map/all_gather | solution.py:18
  275.8 0.8 copy.70
  276.6 9.2 %copy.65 = f32[64,64,256]{1,0,2:T(8,128)} copy(f32[64,64,256]{2,1,0:T(8,128)} %fusion.5) | data formatting | bytes 8388608 | tf_op jit(solution)/shard_map/tsk,kc->tsc/dot_general | solution.py:59
  285.8 0.2 copy.61
  285.9 0.0 collective-permute-done
  285.9 0.2 maximum_convert_fusion
  286.1 1.5 fusion.21
  287.6 0.1 copy.62
  287.8 0.1 copy.64
  287.9 15.4 %fusion.32 = f32[256,2,64]{2,1,0:T(2,128)S(1)} fusion(f32[2,64,256]{1,0,2:T(2,128)S(1)} %copy.64, f32[64,64,256]{1,0,2:T(8,128)} %copy.65), kind=kOutput, calls=%fused_computation.61 | convolution fusion | flops 25165824 | bytes 4456448 | tf_op jit(solution)/shard_map/tsc,bsc->btc/dot_general | solution.py:60
  303.4 4.2 multiply_reduce_fusion.1
  307.6 1.0 copy.68
  308.6 39.9 %all-gather.1 = f32[128,256]{1,0:T(8,128)S(1)} all-gather(f32[16,256]{1,0:T(8,128)S(1)} %copy.68), channel_id=3, replica_groups=mesh['dp'=4,'seq'=8,'tensor'=16] {'seq'}, dimensions={0}, use_global_device_ids=true | all-gather | bytes 147456 | tf_op jit(solution)/shard_map/all_gather | solution.py:18
  348.5 0.1 copy.69
  348.6 1.2 while.25
  348.6 0.6 bitcast_dynamic-update-slice_fusion.2
  349.2 0.6 bitcast_dynamic-update-slice_fusion.2
  349.8 0.9 copy.71
  350.7 0.0 copy-start.6
  350.7 3.7 fusion.12
  354.5 0.1 copy.72
  354.6 0.1 copy.73
  354.7 0.7 fusion.28
  355.5 0.0 all-gather.10.cloned.1.call-update
  355.5 88.6 %all-gather.10.cloned.1.call-done = bf16[128,4096]{0,1:T(8,128)(2,1)} async-done(((bf16[128,256]{0,1:T(8,128)(2,1)}), bf16[128,4096]{0,1:T(8,128)(2,1)}) %all-gather.10.cloned.1.call-update) | async-done | bytes 1048592 | tf_op jit(solution)/shard_map/all_gather | solution.py:90
  444.1 2.4 convolution_convert_fusion.1
  (29 shorter events, 0.1 us)
Async XLA Ops:
  6.5 437.5 %copy-start = (bf16[4096,256]{1,0:T(8,128)(2,1)S(1)}, bf16[4096,256]{1,0:T(8,128)(2,1)}, u32[]{:S(2)}) copy-start(bf16[4096,256]{1,0:T(8,128)(2,1)} %param.17) | copy-start | bytes 6291460
  6.5 3.2 copy-start.4
  6.5 3.2 copy-start.5
  6.5 6.2 %copy-start.3 = (f32[3,7,256]{2,1,0:T(8,128)S(1)}, f32[3,7,256]{2,1,0:T(8,128)}, u32[]{:S(2)}) copy-start(f32[3,7,256]{2,1,0:T(8,128)} %param.13) | copy-start | bytes 64516
  6.5 86.7 %all-gather.6.cloned.1.call-start = ((), (), s32[]{:S(2)}) async-start(), calls=%async_computation | async-start | bytes 1114112 | tf_op jit(solution)/shard_map/all_gather | solution.py:33
  7.3 221.5 %all-gather.8.cloned.1.call-start = ((), (), s32[]{:S(2)}) async-start(), calls=%async_computation.1 | async-start | bytes 7077888 | tf_op jit(solution)/shard_map/all_gather | solution.py:34
  9.7 434.4 %all-gather.10.cloned.1.call-start = ((), (), s32[]{:S(2)}) async-start(), calls=%async_computation.2 | async-start | bytes 1114112 | tf_op jit(solution)/shard_map/all_gather | solution.py:90
  10.0 6.6 %copy-start.1 = (f32[16,256]{0,1:T(8,128)}, f32[16,256]{0,1:T(8,128)S(1)}, u32[]{:S(2)}) copy-start(f32[16,256]{0,1:T(8,128)S(1)} %copy.63) | copy-start | bytes 49156
  10.0 6.6 %copy-start.7 = (f32[64]{0:T(128)}, f32[64]{0:T(128)S(1)}, u32[]{:S(2)}) copy-start(f32[64]{0:T(128)S(1)} %iota_convert_fusion) | copy-start | bytes 772
  234.4 51.6 %collective-permute-start = (bf16[6,3,256]{0,2,1:T(8,128)(2,1)S(1)}, bf16[6,3,256]{0,2,1:T(8,128)(2,1)S(1)}, u32[]{:S(2)}, u32[]{:S(2)}) collective-permute-start(bf16[6,3,256]{0,2,1:T(8,128)(2,1)S(1)} %bitcast.76), channel_id=1, source_target_pairs={{0,16},{16,32},{32,48},{48,64},{64,80},{80,96},{96,112},{1,17},{17... | collective-permute-start | bytes 27656 | tf_op jit(solution)/shard_map/ppermute | solution.py:13
  287.9 15.5 %copy-start.2 = (f32[16,256]{0,1:T(8,128)S(1)}, f32[16,256]{0,1:T(8,128)}, u32[]{:S(2)}) copy-start(f32[16,256]{0,1:T(8,128)} %copy-done.1) | copy-start | bytes 49156
  287.9 15.4 %copy-start.8 = (f32[2]{0:T(128)S(1)}, f32[2]{0:T(128)}, u32[]{:S(2)}) copy-start(f32[2]{0:T(128)} %subtract_multiply_fusion) | copy-start | bytes 28
  287.9 15.4 %copy-start.9 = (f32[64]{0:T(128)S(1)}, f32[64]{0:T(128)}, u32[]{:S(2)}) copy-start(f32[64]{0:T(128)} %broadcast_subtract_fusion) | copy-start | bytes 772
  350.7 4.0 copy-start.6
Sparse Core Ops, SparseCore 0:
  10.5 82.7 all-gather.5
  95.4 133.4 all-gather.7
  355.6 88.4 all-gather.9
where the time goes:
time: 453 us
  waiting for transfers between devices  301 us (66%)
  blocking collectives  80.1 us (18%)
  matrix products  35 us (8%)
  local copies, waits for them, and re-layouts  16.5 us (4%)
  between operations  13.4 us (3%)
  other arithmetic  5.16 us (1%)
    all_gather x1, waiting for transfers between devices, body(): piece = lax.all_gather(in_weight, 'seq', axis=0, tiled=True)  136 us
    all_gather x1, waiting for transfers between devices, body(): lax.all_gather(gated, 'tensor', axis=1, tiled=True)  88.6 us
    all_gather x2, blocking collectives, prefix_2(): gathered = jax.tree.map(lambda a: lax.all_gather(a, axis), part)  80.1 us
    all_gather x1, waiting for transfers between devices, body(): whole_feats = lax.all_gather(features, 'tensor', axis=1, tiled=True)  76.7 us
    dot_general x1, matrix products, body(): inner = jnp.einsum('tsc,bsc->btc', toeplitz, pieces, precision=precise)  15.4 us
    dot_general x1, local copies, waits for them, and re-layouts, body(): toeplitz = jnp.einsum('tsk,kc->tsc', select, kernel, precision=precise)  9.17 us
  transfers between devices with their start and end apart: 4, of which 3 were waited for; matrix products, arithmetic and copies ran while one was open for 4% of the time, Pallas kernels for 0%

commit v1 on v0

--- a/solution.py
+++ b/solution.py
@@ -31,7 +31,9 @@
     channels = in_weight.shape[2]
     taps_count = short_taps.shape[1]
     whole_feats = lax.all_gather(features, "tensor", axis=1, tiled=True)
-    piece = lax.all_gather(in_weight, "seq", axis=0, tiled=True)
+    piece = jnp.concatenate(
+        lax.all_to_all(jnp.stack([in_weight] * lax.axis_size("seq")), "seq", 0, 0), axis=0
+    )
     count = piece.shape[0]
     projected = jnp.dot(
         whole_feats, piece.reshape(count, 3 * channels), preferred_element_type=jnp.float32

time: 453 us -> 551 us (1.22)
  waiting for transfers between devices: 301 us -> 372 us
  local copies, waits for them, and re-layouts: 16.5 us -> 30.3 us
  starting transfers between devices: 1.42 us -> 14.6 us
    all_to_all x0 -> x1, waiting for transfers between devices: none -> 283 us  [body(): lax.all_to_all(jnp.stack([in_weight] * lax.axis_size('seq')), 'seq', 0, 0)]
    all_gather x1 -> x0, waiting for transfers between devices: 136 us -> none  [body(): piece = lax.all_gather(in_weight, 'seq', axis=0, tiled=True)]
    all_gather x1, waiting for transfers between devices: 76.7 us -> 0.01 us  [body(): whole_feats = lax.all_gather(features, 'tensor', axis=1, tiled=True)]
    all_to_all x0 -> x1, starting transfers between devices: none -> 13.2 us  [body(): lax.all_to_all(jnp.stack([in_weight] * lax.axis_size('seq')), 'seq', 0, 0)]
    all_to_all x0 -> x1, local copies, waits for them, and re-layouts: none -> 6.35 us  [body(): lax.all_to_all(jnp.stack([in_weight] * lax.axis_size('seq')), 'seq', 0, 0)]
    unnamed x26 -> x17, local copies, waits for them, and re-layouts: 2.49 us -> 8.53 us
  transfers between devices with their start and end apart: 4 -> 4, of which waited for: 3 -> 2; matrix products, arithmetic and copies ran while one was open for 4% -> 5% of each run, Pallas kernels for 0% -> 0%
where the time goes in v1:
time: 551 us; the launch traced here: 550 us
  waiting for transfers between devices  372 us (68%)
  blocking collectives  80.1 us (15%)
  matrix products  34.9 us (6%)
  local copies, waits for them, and re-layouts  30.3 us (5%)
  starting transfers between devices  14.6 us (3%)
  between operations  13.6 us (2%)
    all_to_all x1, waiting for transfers between devices, body(): lax.all_to_all(jnp.stack([in_weight] * lax.axis_size('seq')), 'seq', 0, 0)  283 us
    all_gather x1, waiting for transfers between devices, body(): lax.all_gather(gated, 'tensor', axis=1, tiled=True)  89.2 us
    all_gather x2, blocking collectives, prefix_2(): gathered = jax.tree.map(lambda a: lax.all_gather(a, axis), part)  80.1 us
    dot_general x1, matrix products, body(): inner = jnp.einsum('tsc,bsc->btc', toeplitz, pieces, precision=precise)  15.4 us
    all_to_all x1, starting transfers between devices, body(): lax.all_to_all(jnp.stack([in_weight] * lax.axis_size('seq')), 'seq', 0, 0)  13.2 us
  transfers between devices with their start and end apart: 4, of which 2 were waited for; matrix products, arithmetic and copies ran while one was open for 5% of the time, Pallas kernels for 0%

profile of v1, /device:TPU:1, one launch (start us, length us, event | category | flops | bytes accessed | tf_op | source)
XLA Modules:
  0.0 550.1 jit_solution(12459044475568966472)
XLA Ops:
  6.5 0.0 copy-start
  6.5 1.6 copy.62
  8.1 3.3 stack.2
  11.4 0.0 copy-start.2
  11.4 0.0 copy-start.3
  11.4 13.2 %all-to-all-start = ((bf16[8,512,3,256]{1,3,2,0:T(8,128)(2,1)}), bf16[8,512,3,256]{1,3,2,0:T(8,128)(2,1)}, u32[]{:S(2)}, u32[]{:S(2)}) async-start(bf16[8,512,3,256]{1,3,2,0:T(8,128)(2,1)} %stack.2), calls=%async_computation | async-start | bytes 12582912 | tf_op jit(solution)/shard_map/all_to_all | solution.py:35
  24.6 0.0 all-gather.5.cloned.1.call-start
  24.7 0.7 all-gather.5.cloned.1.call-update
  25.4 0.0 all-gather.7.cloned.1.call-start
  25.4 0.0 copy-done.2
  25.4 0.0 copy-done.3
  25.5 0.1 copy.94
  25.6 0.1 copy.67
  25.7 1.6 multiply_reduce_fusion
  27.3 0.0 copy-done.1
  27.4 3.8 fusion.5
  31.2 282.6 %all-to-all-done = bf16[8,512,3,256]{1,3,2,0:T(8,128)(2,1)} async-done(((bf16[8,512,3,256]{1,3,2,0:T(8,128)(2,1)}), bf16[8,512,3,256]{1,3,2,0:T(8,128)(2,1)}, u32[]{:S(2)}, u32[]{:S(2)}) %all-to-all-start) | async-done | bytes 6291488 | tf_op jit(solution)/shard_map/all_to_all | solution.py:35
  313.8 6.4 %copy.63 = bf16[8,512,3,256]{1,0,3,2:T(8,128)(2,1)S(1)} copy(bf16[8,512,3,256]{1,3,2,0:T(8,128)(2,1)} %all-to-all-done) | data formatting | bytes 12582912 | tf_op jit(solution)/shard_map/all_to_all | solution.py:35
  320.1 6.8 %copy.95 = bf16[96,8,8,512]{3,1,2,0:T(8,128)(2,1)} copy(bf16[96,8,8,512]{3,2,1,0:T(8,128)(2,1)S(1)} %bitcast.75) | data formatting | bytes 12582912
  327.0 5.3 convolution_convert_fusion
  332.3 0.2 copy.85
  332.5 1.3 collective-permute-start
  333.8 40.2 %all-gather = f32[128,256]{1,0:T(8,128)S(1)} all-gather(f32[16,256]{1,0:T(8,128)S(1)} %get-tuple-element.136), channel_id=2, replica_groups=mesh['dp'=4,'seq'=8,'tensor'=16] {'seq'}, dimensions={0}, use_global_device_ids=true | all-gather | bytes 147456 | tf_op jit(solution)/shard_map/all_gather | solution.py:18
  374.0 0.7 copy.74
  374.7 9.2 %copy.69 = f32[64,64,256]{1,0,2:T(8,128)} copy(f32[64,64,256]{2,1,0:T(8,128)} %fusion.5) | data formatting | bytes 8388608 | tf_op jit(solution)/shard_map/tsk,kc->tsc/dot_general | solution.py:61
  383.9 0.2 copy.65
  384.1 0.0 collective-permute-done
  384.1 0.2 maximum_convert_fusion
  384.3 1.5 fusion.21
  385.8 0.1 copy.66
  385.9 0.1 copy.68
  386.0 15.4 %fusion.32 = f32[256,2,64]{2,1,0:T(2,128)S(1)} fusion(f32[2,64,256]{1,0,2:T(2,128)S(1)} %copy.68, f32[64,64,256]{1,0,2:T(8,128)} %copy.69), kind=kOutput, calls=%fused_computation.61 | convolution fusion | flops 25165824 | bytes 4456448 | tf_op jit(solution)/shard_map/tsc,bsc->btc/dot_general | solution.py:62
  401.4 4.3 multiply_reduce_fusion.1
  405.7 0.1 copy.72
  405.7 39.9 %all-gather.1 = f32[128,256]{1,0:T(8,128)S(1)} all-gather(f32[16,256]{1,0:T(8,128)S(1)} %copy.72), channel_id=3, replica_groups=mesh['dp'=4,'seq'=8,'tensor'=16] {'seq'}, dimensions={0}, use_global_device_ids=true | all-gather | bytes 147456 | tf_op jit(solution)/shard_map/all_gather | solution.py:18
  445.7 1.0 copy.73
  446.7 0.1 while.25
  446.8 0.1 copy.75
  446.9 0.0 copy-start.4
  447.0 3.7 fusion.12
  450.7 0.1 copy.76
  450.8 0.1 copy.77
  450.9 0.0 copy-done.4
  450.9 0.7 fusion.28
  451.6 0.0 all-gather.7.cloned.1.call-update
  451.7 89.2 %all-gather.7.cloned.1.call-done = bf16[128,4096]{0,1:T(8,128)(2,1)} async-done(((bf16[128,256]{0,1:T(8,128)(2,1)}), bf16[128,4096]{0,1:T(8,128)(2,1)}) %all-gather.7.cloned.1.call-update) | async-done | bytes 1048592 | tf_op jit(solution)/shard_map/all_gather | solution.py:92
  540.9 0.0 copy-done
  540.9 2.4 convolution_convert_fusion.1
  (21 shorter events, 0.1 us)
Async XLA Ops:
  6.5 534.3 %copy-start = (bf16[4096,256]{1,0:T(8,128)(2,1)S(1)}, bf16[4096,256]{1,0:T(8,128)(2,1)}, u32[]{:S(2)}) copy-start(bf16[4096,256]{1,0:T(8,128)(2,1)} %param.17) | copy-start | bytes 6291460
  11.4 14.0 %copy-start.2 = (f32[16,256]{1,0:T(8,128)S(1)}, f32[16,256]{1,0:T(8,128)}, u32[]{:S(2)}) copy-start(f32[16,256]{1,0:T(8,128)} %param.14) | copy-start | bytes 49156
  11.4 14.0 %copy-start.3 = (f32[16,256]{1,0:T(8,128)S(1)}, f32[16,256]{1,0:T(8,128)}, u32[]{:S(2)}) copy-start(f32[16,256]{1,0:T(8,128)} %param.15) | copy-start | bytes 49156
  11.4 15.9 %copy-start.1 = (f32[3,7,256]{2,1,0:T(8,128)S(1)}, f32[3,7,256]{2,1,0:T(8,128)}, u32[]{:S(2)}) copy-start(f32[3,7,256]{2,1,0:T(8,128)} %param.13) | copy-start | bytes 64516
  11.4 302.4 %all-to-all-start = ((bf16[8,512,3,256]{1,3,2,0:T(8,128)(2,1)}), bf16[8,512,3,256]{1,3,2,0:T(8,128)(2,1)}, u32[]{:S(2)}, u32[]{:S(2)}) async-start(bf16[8,512,3,256]{1,3,2,0:T(8,128)(2,1)} %stack.2), calls=%async_computation | async-start | bytes 12582912 | tf_op jit(solution)/shard_map/all_to_all | solution.py:35
  24.6 302.3 %all-gather.5.cloned.1.call-start = ((), (), s32[]{:S(2)}) async-start(), calls=%async_computation.1 | async-start | bytes 1114112 | tf_op jit(solution)/shard_map/all_gather | solution.py:33
  25.4 515.5 %all-gather.7.cloned.1.call-start = ((), (), s32[]{:S(2)}) async-start(), calls=%async_computation.2 | async-start | bytes 1114112 | tf_op jit(solution)/shard_map/all_gather | solution.py:92
  332.5 51.6 %collective-permute-start = (bf16[6,3,256]{0,2,1:T(8,128)(2,1)S(1)}, bf16[6,3,256]{0,2,1:T(8,128)(2,1)S(1)}, u32[]{:S(2)}, u32[]{:S(2)}) collective-permute-start(bf16[6,3,256]{0,2,1:T(8,128)(2,1)S(1)} %bitcast.81), channel_id=1, source_target_pairs={{0,16},{16,32},{32,48},{48,64},{64,80},{80,96},{96,112},{1,17},{17... | collective-permute-start | bytes 27656 | tf_op jit(solution)/shard_map/ppermute | solution.py:13
  446.9 3.9 copy-start.4
Sparse Core Ops, SparseCore 0:
  28.6 139.4 all-gather.4
  451.8 89.0 all-gather.6
